TPU v7x, 512 devices: a whole 4x4x16 slice. The times are simulated.
512 devices in a mesh: grp: 4 (over x), ch: 128 (over y, z, core).
Axes of the slice: x: 4, y: 4, z: 16, core: 2. Of those that a mesh axis runs over, the one named last changes fastest.
Arguments:
- raw_strain: bfloat16 [4, 7680, 8192], P('grp', 'ch'), may hold values from -6 to 6
- window_valid: int32 [4, 8192], P(None, 'ch'), may hold values 0 or 1
- band_first: int32 [8192], P('ch'), may hold values from 1 to 17
- band_end: int32 [8192], P('ch'), may hold values from 34 to 128
Outputs:
- stacked: float32 [8192, 32, 128], P('ch')
All inputs are finite; a program needn't handle non-finite values. No bound on the sum of `window_valid` on one device may be relied on, other than what follows from the above.
Results may differ from a plain program's by a relative error of at most 0.008.
Values may be sent and summed in bfloat16 or wider, within the bound.
No kernel may reach another device: no remote copies, remote signals or barrier semaphores. Data moves between devices by JAX's collectives and lax.ppermute only.
A program may use at most 64 MiB of HBM per device.

v0:
```python
import jax
import jax.numpy as jnp
from jax import lax
from jax.sharding import PartitionSpec as P

NT = 7680
F = 384
KH = 128
SMOOTH = 65
LAGS = 32
LAG_STEP = 10
eps_white = 1e-06


def from_behind(array, axis, by):
    count = lax.axis_size(axis)
    pairs = [(i, i + by) for i in range(count) if 0 <= i + by < count]
    return lax.ppermute(array, axis, pairs)


def dft_matrix(samples, bin_count):
    sample_index = jnp.arange(samples, dtype=jnp.int32)[:, None]
    orders = jnp.arange(1, bin_count + 1, dtype=jnp.int32)[None, :]
    phases = (sample_index * orders % samples).astype(jnp.float32) * (2.0 * jnp.pi / samples)
    return jnp.concatenate([jnp.cos(phases), -jnp.sin(phases)], axis=1).astype(jnp.bfloat16)


def smoothing_matrix(bin_count, window_bins):
    row_index = jnp.arange(bin_count, dtype=jnp.int32)[:, None]
    col_index = jnp.arange(bin_count, dtype=jnp.int32)[None, :]
    distance = (row_index - col_index) % bin_count
    halfwidth = window_bins // 2
    inside = (distance <= halfwidth) | (distance >= bin_count - halfwidth)
    return inside.astype(jnp.float32)


def whiten(spectra, bin_count, window_bins):
    real_part = spectra[..., :bin_count]
    imag_part = spectra[..., bin_count:]
    magnitude = jnp.sqrt(real_part * real_part + imag_part * imag_part)
    averaged = (
        jnp.dot(
            magnitude,
            smoothing_matrix(bin_count, window_bins),
            precision=lax.Precision.HIGHEST,
            preferred_element_type=jnp.float32,
        )
        / window_bins
    )
    factor = 1.0 / (averaged + eps_white)
    return (spectra * jnp.concatenate([factor, factor], axis=-1)).astype(jnp.bfloat16)


def rotated(extended, lag_first, lag_count, lag_step, samples, bin_count):
    orders = jnp.arange(1, bin_count + 1, dtype=jnp.int32)[None, :]
    shifts = ((lag_first + jnp.arange(lag_count, dtype=jnp.int32)) * lag_step)[:, None]
    phases = (shifts * orders % samples).astype(jnp.float32) * (2.0 * jnp.pi / samples)
    cosine = jnp.cos(phases)
    sine_part = jnp.sin(phases)
    real_part = extended[..., :bin_count].astype(jnp.float32)[:, :, None, :]
    imag_part = extended[..., bin_count:].astype(jnp.float32)[:, :, None, :]
    rotated_real = real_part * cosine + imag_part * sine_part
    rotated_imag = imag_part * cosine - real_part * sine_part
    return jnp.concatenate([rotated_real, rotated_imag], axis=-1).astype(jnp.bfloat16)


def diagonal_band(matrix, offsets):
    row_count, col_count = matrix.shape
    flat_rows = matrix.reshape(row_count * col_count)
    padded = jnp.concatenate([flat_rows, jnp.zeros((row_count,), matrix.dtype)])
    skewed = padded.reshape(row_count, col_count + 1)
    return skewed[:, :offsets]


def lag_band(block_full, offsets):
    banded = jax.vmap(lambda matrix: diagonal_band(matrix, offsets))(block_full)
    return jnp.transpose(banded, (1, 0, 2))


def normalise(lagged, pair_counts, band_lows, band_highs, bin_count):
    offsets = jnp.arange(lagged.shape[2], dtype=jnp.int32)[None, :]
    in_band = (offsets >= band_lows[:, None]) & (offsets < band_highs[:, None])
    weights = jnp.where(
        in_band, 1.0 / jnp.sqrt(float(bin_count) * jnp.maximum(pair_counts, 1.0)), 0.0
    )
    return lagged * weights[:, None, :]


def local(raw_strain, window_valid, band_first, band_end):
    dft_table = dft_matrix(NT, F)
    spectra = jnp.einsum(
        "nta,tf->naf",
        lax.all_to_all(raw_strain, "ch", split_axis=2, concat_axis=1, tiled=True),
        dft_table,
        preferred_element_type=jnp.float32,
    )
    whitened = whiten(spectra, F, SMOOTH)
    valid_flags = window_valid.astype(jnp.bfloat16)
    group_index = lax.axis_index("grp")
    own_flags = lax.dynamic_slice_in_dim(valid_flags, group_index, 1, 0)
    whitened = whitened * own_flags[:, :, None]
    channels_here = whitened.shape[1]
    blocks_up = (KH + channels_here - 1) // channels_here
    white_parts = [whitened]
    flag_parts = [valid_flags]
    for neighbour in range(1, blocks_up + 1):
        moved_white, moved_flags = from_behind((whitened, valid_flags), "ch", -neighbour)
        white_parts.append(moved_white)
        flag_parts.append(moved_flags)
    extended = jnp.concatenate(white_parts, axis=1)
    ext_flags = jnp.concatenate(flag_parts, axis=1)
    pair_full = jnp.einsum("na,nb->ab", valid_flags, ext_flags, preferred_element_type=jnp.float32)
    pair_counts = diagonal_band(pair_full, KH)
    turned = rotated(extended, -(LAGS // 2), LAGS, LAG_STEP, NT, F)
    block_full = jnp.einsum("nak,nblk->lab", whitened, turned, preferred_element_type=jnp.float32)
    lagged = lax.psum(lag_band(block_full, KH).astype(jnp.bfloat16), "grp").astype(jnp.float32)
    return normalise(lagged, pair_counts, band_first, band_end, F)


def solution(mesh):
    placed = (P("grp", "ch", None), P(None, "ch"), P("ch"), P("ch"))
    return jax.shard_map(
        local, mesh=mesh, in_specs=placed, out_specs=P("ch", None, None), check_vma=False
    )
```

profile of v0, /device:TPU:8, one launch (start us, length us, event | category | flops | bytes accessed | tf_op | source)
XLA Modules:
  0.0 264.4 jit_solution(14576265745442213151)
XLA Ops:
  6.5 9.2 %copy.8 = bf16[1,60,8192]{1,0,2:T(2,128)(2,1)} copy(bf16[1,60,8192]{2,1,0:T(8,128)(2,1)} %param.4) | data formatting | bytes 1966080 | tf_op args[0]
  15.7 0.0 copy-start
  15.7 0.5 broadcast.138
  16.3 45.2 %reduce = bf16[8192,60]{1,0:T(8,128)(2,1)S(1)} reduce(bf16[8192,1,60]{2,1,0:T(2,128)(2,1)} %bitcast.40, bf16[]{:T(256)} %broadcast.138), dimensions={1}, to_apply=%bitcast.36.reduce_sub_computation | reduce | bytes 1966082
  61.5 6.4 %reshape.150 = bf16[128,2,1920]{2,1,0:T(2,128)(2,1)} reshape(bf16[8192,60]{1,0:T(8,128)(2,1)S(1)} %reduce) | data formatting | bytes 1966080
  67.9 19.6 %all-to-all-start = ((bf16[128,2,1920]{2,1,0:T(2,128)(2,1)}), bf16[128,2,1920]{2,1,0:T(2,128)(2,1)S(1)}, u32[]{:S(2)}, u32[]{:S(2)}) async-start(bf16[128,2,1920]{2,1,0:T(2,128)(2,1)} %reshape.150), calls=%async_computation | async-start | bytes 1966080 | tf_op jit(solution)/shard_map/all_to_all | solution.py:93
  87.5 0.2 all-reduce.4.cloned.1.call-start
  87.7 0.0 copy-done
  87.8 50.6 %cosine_convert_fusion = (bf16[7680,384]{1,0:T(8,128)(2,1)}, bf16[7680,384]{1,0:T(8,128)(2,1)}) fusion(s32[384]{0:T(512)S(1)} %iota_add_fusion), kind=kLoop, calls=%fused_computation.8 | loop fusion | flops 35389440 | bytes 11798016 | tf_op jit(solution)/shard_map/convert.10
  138.4 2.0 all-to-all-done
  140.4 9.5 %reshape.151 = bf16[8192,1,60]{2,1,0:T(2,128)(2,1)} reshape(bf16[128,2,1920]{2,1,0:T(2,128)(2,1)S(1)} %all-to-all-done) | data formatting | bytes 1966080
  149.9 8.4 %copy.9 = bf16[1,60,8192]{2,1,0:T(8,128)(2,1)S(1)} copy(bf16[1,60,8192]{1,0,2:T(2,128)(2,1)} %bitcast.41) | data formatting | bytes 1966080 | tf_op jit(solution)/shard_map/all_to_all | solution.py:93
  158.3 3.5 %all_to_all.12 = bf16[1,60,128,64]{3,2,1,0:T(8,128)(2,1)} reshape(bf16[1,60,8192]{2,1,0:T(8,128)(2,1)S(1)} %copy.9) | data formatting | bytes 1966080 | tf_op jit(solution)/shard_map/all_to_all | solution.py:93
  161.8 4.7 %copy.10 = bf16[1,128,60,64]{2,1,3,0:T(8,128)(2,1)S(1)} copy(bf16[1,128,60,64]{3,1,2,0:T(8,128)(2,1)} %bitcast.42) | data formatting | bytes 1966080 | tf_op jit(solution)/shard_map/all_to_all | solution.py:93
  166.5 4.1 %reshape.141 = bf16[7680,64]{0,1:T(8,128)(2,1)S(1)} reshape(bf16[1,128,60,64]{2,1,3,0:T(8,128)(2,1)S(1)} %copy.10) | data formatting | bytes 1966080 | tf_op jit(solution)/shard_map/reshape
  170.6 5.6 %fusion.2 = f32[768,64]{0,1:T(8,128)S(1)} fusion(bf16[7680,64]{0,1:T(8,128)(2,1)S(1)} %reshape.141, bf16[7680,384]{1,0:T(8,128)(2,1)} %get-tuple-element.12, bf16[7680,384]{1,0:T(8,128)(2,1)} %get-tuple-element.11), kind=kOutput, calls=%fused_computation.3 | convolution fusion | flops 778567680 | bytes 12976128 | tf_op jit(solution)/shard_map/nta,tf->naf/dot_general | solution.py:91
  176.2 0.7 fusion.20
  176.9 0.1 fusion.35
  177.0 2.6 collective-permute-start.1
  179.5 3.0 %collective-permute-start = (bf16[1,64,768]{2,1,0:T(8,128)(2,1)S(1)}, bf16[1,64,768]{2,1,0:T(8,128)(2,1)S(1)}, u32[]{:S(2)}, u32[]{:S(2)}) collective-permute-start(bf16[1,64,768]{2,1,0:T(8,128)(2,1)S(1)} %bitcast.44), channel_id=1, source_target_pairs={{1,0},{2,1},{3,2},{4,3},{5,4},{6,5},{7,6},{8,7},{9,8},{10,9},{11,1... | collective-permute-start | bytes 294920 | tf_op jit(solution)/shard_map/ppermute | solution.py:18
  182.6 0.3 fusion.46
  182.9 0.6 collective-permute-done.1
  183.5 1.1 collective-permute-done
  184.6 2.6 add_convert_fusion
  187.2 2.9 %fusion.16 = bf16[32,64,192]{1,0,2:T(8,128)(2,1)S(1)} fusion(bf16[192,32,384]{2,1,0:T(8,128)(2,1)S(1)} %get-tuple-element.6, bf16[192,32,384]{2,1,0:T(8,128)(2,1)S(1)} %get-tuple-element.5, bf16[64,768]{1,0:T(8,128)(2,1)S(1)} %fusion.35), kind=kOutput, calls=%fused_computation.20 | convolution fusion | flops 623247360 | bytes 10321920 | tf_op jit(solution)/shard_map/nak,nblk->lab/dot_general | solution.py:115
  190.1 0.0 copy-start.1
  190.2 0.0 copy-start.2
  190.2 1.4 copy.11
  191.5 1.1 reshape.143
  192.7 0.1 concatenate.31
  192.7 3.2 %reshape.144 = bf16[32,64,193]{2,1,0:T(8,128)(2,1)S(1)} reshape(bf16[32,12352]{1,0:T(8,128)(2,1)S(1)} %concatenate.31) | data formatting | bytes 1581056 | tf_op jit(solution)/shard_map/vmap()/reshape | solution.py:71
  195.9 0.9 slice_bitcast_fusion
  196.8 0.0 all-reduce.4.cloned.1.call-update
  196.9 3.8 %collective-permute-start.3 = (bf16[4,64]{1,0:T(4,128)(2,1)S(1)}, bf16[4,64]{1,0:T(4,128)(2,1)S(1)}, u32[]{:S(2)}, u32[]{:S(2)}) collective-permute-start(bf16[4,64]{1,0:T(4,128)(2,1)S(1)} %convert_element_type.45), channel_id=1, source_target_pairs={{2,0},{3,1},{4,2},{5,3},{6,4},{7,5},{8,6},{9,7},{10,8},{11,9},{12,... | collective-permute-start | bytes 1544 | tf_op jit(solution)/shard_map/ppermute | solution.py:18
  200.7 4.0 %collective-permute-start.2 = (bf16[4,64]{1,0:T(4,128)(2,1)S(1)}, bf16[4,64]{1,0:T(4,128)(2,1)S(1)}, u32[]{:S(2)}, u32[]{:S(2)}) collective-permute-start(bf16[4,64]{1,0:T(4,128)(2,1)S(1)} %convert_element_type.45), channel_id=1, source_target_pairs={{1,0},{2,1},{3,2},{4,3},{5,4},{6,5},{7,6},{8,7},{9,8},{10,9},{11,1... | collective-permute-start | bytes 1544 | tf_op jit(solution)/shard_map/ppermute | solution.py:18
  204.7 0.0 collective-permute-done.3
  204.7 1.3 collective-permute-done.2
  205.9 0.2 convolution_bitcast_fusion
  206.1 0.1 reshape.145
  206.3 0.2 reshape.146
  206.5 0.0 copy-done.1
  206.5 0.0 copy-done.2
  206.5 0.1 fusion.50
  206.6 48.2 %all-reduce.4.cloned.1.call-done = bf16[64,32,128]{2,0,1:T(8,128)(2,1)} async-done(((bf16[64,32,128]{2,0,1:T(8,128)(2,1)}), bf16[64,32,128]{2,0,1:T(8,128)(2,1)}) %all-reduce.4.cloned.1.call-update) | async-done | bytes 524304 | tf_op jit(solution)/shard_map/psum | solution.py:116
  254.8 1.2 convert_multiply_fusion
  256.0 1.6 copy.12
  (7 shorter events, 0.1 us)
Async XLA Ops:
  15.7 72.0 %copy-start = (s32[4,64]{1,0:T(4,128)S(1)}, s32[4,64]{1,0:T(4,128)}, u32[]{:S(2)}) copy-start(s32[4,64]{1,0:T(4,128)} %param.5) | copy-start | bytes 3076
  67.9 72.5 %all-to-all-start = ((bf16[128,2,1920]{2,1,0:T(2,128)(2,1)}), bf16[128,2,1920]{2,1,0:T(2,128)(2,1)S(1)}, u32[]{:S(2)}, u32[]{:S(2)}) async-start(bf16[128,2,1920]{2,1,0:T(2,128)(2,1)} %reshape.150), calls=%async_computation | async-start | bytes 1966080 | tf_op jit(solution)/shard_map/all_to_all | solution.py:93
  87.5 167.3 %all-reduce.4.cloned.1.call-start = ((), (), s32[]{:S(2)}) async-start(), calls=%async_computation.1 | async-start | bytes 1048576 | tf_op jit(solution)/shard_map/psum | solution.py:116
  177.0 6.5 %collective-permute-start.1 = (bf16[1,64,768]{2,1,0:T(8,128)(2,1)S(1)}, bf16[1,64,768]{2,1,0:T(8,128)(2,1)S(1)}, u32[]{:S(2)}, u32[]{:S(2)}) collective-permute-start(bf16[1,64,768]{2,1,0:T(8,128)(2,1)S(1)} %bitcast.43), channel_id=1, source_target_pairs={{2,0},{3,1},{4,2},{5,3},{6,4},{7,5},{8,6},{9,7},{10,8},{11,9},{12,... | collective-permute-start | bytes 294920 | tf_op jit(solution)/shard_map/ppermute | solution.py:18
  179.5 5.0 %collective-permute-start = (bf16[1,64,768]{2,1,0:T(8,128)(2,1)S(1)}, bf16[1,64,768]{2,1,0:T(8,128)(2,1)S(1)}, u32[]{:S(2)}, u32[]{:S(2)}) collective-permute-start(bf16[1,64,768]{2,1,0:T(8,128)(2,1)S(1)} %bitcast.44), channel_id=1, source_target_pairs={{1,0},{2,1},{3,2},{4,3},{5,4},{6,5},{7,6},{8,7},{9,8},{10,9},{11,1... | collective-permute-start | bytes 294920 | tf_op jit(solution)/shard_map/ppermute | solution.py:18
  190.1 16.3 %copy-start.1 = (s32[64]{0:T(128)S(1)}, s32[64]{0:T(128)}, u32[]{:S(2)}) copy-start(s32[64]{0:T(128)} %param.7) | copy-start | bytes 772
  190.2 16.3 %copy-start.2 = (s32[64]{0:T(128)S(1)}, s32[64]{0:T(128)}, u32[]{:S(2)}) copy-start(s32[64]{0:T(128)} %param.6) | copy-start | bytes 772
  196.9 7.8 %collective-permute-start.3 = (bf16[4,64]{1,0:T(4,128)(2,1)S(1)}, bf16[4,64]{1,0:T(4,128)(2,1)S(1)}, u32[]{:S(2)}, u32[]{:S(2)}) collective-permute-start(bf16[4,64]{1,0:T(4,128)(2,1)S(1)} %convert_element_type.45), channel_id=1, source_target_pairs={{2,0},{3,1},{4,2},{5,3},{6,4},{7,5},{8,6},{9,7},{10,8},{11,9},{12,... | collective-permute-start | bytes 1544 | tf_op jit(solution)/shard_map/ppermute | solution.py:18
  200.7 5.2 %collective-permute-start.2 = (bf16[4,64]{1,0:T(4,128)(2,1)S(1)}, bf16[4,64]{1,0:T(4,128)(2,1)S(1)}, u32[]{:S(2)}, u32[]{:S(2)}) collective-permute-start(bf16[4,64]{1,0:T(4,128)(2,1)S(1)} %convert_element_type.45), channel_id=1, source_target_pairs={{1,0},{2,1},{3,2},{4,3},{5,4},{6,5},{7,6},{8,7},{9,8},{10,9},{11,1... | collective-permute-start | bytes 1544 | tf_op jit(solution)/shard_map/ppermute | solution.py:18
Sparse Core Ops, SparseCore 0:
  197.0 57.7 all-reduce.3
where the time goes:
time: 265 us; the launch traced here: 264 us
  other arithmetic  100 us (38%)
  local copies, waits for them, and re-layouts  54.9 us (21%)
  waiting for transfers between devices  53.2 us (20%)
  starting transfers between devices  33.2 us (13%)
  between operations  13.7 us (5%)
  matrix products  9.39 us (4%)
    another operation x2, other arithmetic  53.2 us
    psum x1, waiting for transfers between devices, local(): lax.psum(lag_band(block_full, KH).astype(jnp.bfloat16), 'grp')  48.2 us
    unnamed x1, other arithmetic  45.2 us
    unnamed x10, local copies, waits for them, and re-layouts  25.6 us
    all_to_all x1, starting transfers between devices, local(): lax.all_to_all(raw_strain, 'ch', split_axis=2, concat_axis=1, tiled=True)  19.6 us
    all_to_all x3, local copies, waits for them, and re-layouts, local(): lax.all_to_all(raw_strain, 'ch', split_axis=2, concat_axis=1, tiled=True)  16.6 us
    ppermute x4, starting transfers between devices, from_behind(): return lax.ppermute(array, axis, pairs)  13.4 us
    dot_general x1, matrix products, local(): jnp.einsum('nta,tf->naf', lax.all_to_all(raw_strain, 'ch', split_axis=2,...  5.6 us
  transfers between devices with their start and end apart: 6, of which 5 were waited for; matrix products, arithmetic and copies ran while one was open for 19% of the time, Pallas kernels for 0%

commit v1 on v0

--- a/solution.py
+++ b/solution.py
@@ -113,7 +113,9 @@
     pair_counts = diagonal_band(pair_full, KH)
     turned = rotated(extended, -(LAGS // 2), LAGS, LAG_STEP, NT, F)
     block_full = jnp.einsum("nak,nblk->lab", whitened, turned, preferred_element_type=jnp.float32)
-    lagged = lax.psum(lag_band(block_full, KH).astype(jnp.bfloat16), "grp").astype(jnp.float32)
+    lagged = jnp.sum(
+        lax.all_gather(lag_band(block_full, KH).astype(jnp.bfloat16), "grp"), axis=0
+    ).astype(jnp.float32)
     return normalise(lagged, pair_counts, band_first, band_end, F)
 
 

time: 265 us -> 247 us (0.932)
  the two profiles are of different devices: /device:TPU:8 before, /device:TPU:1 now
where the time goes in v1:
time: 247 us; the launch traced here: 246 us
  other arithmetic  101 us (41%)
  local copies, waits for them, and re-layouts  54.9 us (22%)
  waiting for transfers between devices  37.9 us (15%)
  starting transfers between devices  29.2 us (12%)
  between operations  13.7 us (6%)
  matrix products  9.39 us (4%)
    another operation x2, other arithmetic  53.2 us
    unnamed x1, other arithmetic  45.2 us
    all_gather x1, waiting for transfers between devices, local(): lax.all_gather(lag_band(block_full, KH).astype(jnp.bfloat16), 'grp')  30.2 us
    unnamed x10, local copies, waits for them, and re-layouts  25.6 us
    all_to_all x1, starting transfers between devices, local(): lax.all_to_all(raw_strain, 'ch', split_axis=2, concat_axis=1, tiled=True)  20.6 us
    all_to_all x3, local copies, waits for them, and re-layouts, local(): lax.all_to_all(raw_strain, 'ch', split_axis=2, concat_axis=1, tiled=True)  16.6 us
    ppermute x4, starting transfers between devices, from_behind(): return lax.ppermute(array, axis, pairs)  8.39 us
    ppermute x4, waiting for transfers between devices, from_behind(): return lax.ppermute(array, axis, pairs)  6.98 us
  transfers between devices with their start and end apart: 6, of which 5 were waited for; matrix products, arithmetic and copies ran while one was open for 21% of the time, Pallas kernels for 0%

profile of v1, /device:TPU:1, one launch (start us, length us, event | category | flops | bytes accessed | tf_op | source)
XLA Modules:
  0.0 246.1 jit_solution(7240505289374403999)
XLA Ops:
  6.5 9.2 %copy.7 = bf16[1,60,8192]{1,0,2:T(2,128)(2,1)} copy(bf16[1,60,8192]{2,1,0:T(8,128)(2,1)} %param.4) | data formatting | bytes 1966080 | tf_op args[0]
  15.7 0.0 copy-start
  15.7 0.5 broadcast.138
  16.3 45.2 %reduce.1 = bf16[8192,60]{1,0:T(8,128)(2,1)S(1)} reduce(bf16[8192,1,60]{2,1,0:T(2,128)(2,1)} %bitcast.41, bf16[]{:T(256)} %broadcast.138), dimensions={1}, to_apply=%bitcast.37.reduce_sub_computation | reduce | bytes 1966082
  61.5 6.4 %reshape.151 = bf16[128,2,1920]{2,1,0:T(2,128)(2,1)} reshape(bf16[8192,60]{1,0:T(8,128)(2,1)S(1)} %reduce.1) | data formatting | bytes 1966080
  67.9 20.6 %all-to-all-start = ((bf16[128,2,1920]{2,1,0:T(2,128)(2,1)}), bf16[128,2,1920]{2,1,0:T(2,128)(2,1)S(1)}, u32[]{:S(2)}, u32[]{:S(2)}) async-start(bf16[128,2,1920]{2,1,0:T(2,128)(2,1)} %reshape.151), calls=%async_computation | async-start | bytes 1966080 | tf_op jit(solution)/shard_map/all_to_all | solution.py:93
  88.4 0.2 all-gather.3.cloned.1.call-start
  88.7 0.0 copy-done
  88.7 50.6 %cosine_convert_fusion = (bf16[7680,384]{1,0:T(8,128)(2,1)}, bf16[7680,384]{1,0:T(8,128)(2,1)}) fusion(s32[384]{0:T(512)S(1)} %iota_add_fusion), kind=kLoop, calls=%fused_computation.8 | loop fusion | flops 35389440 | bytes 11798016 | tf_op jit(solution)/shard_map/convert.11
  139.3 0.7 all-to-all-done
  140.1 9.5 %reshape.152 = bf16[8192,1,60]{2,1,0:T(2,128)(2,1)} reshape(bf16[128,2,1920]{2,1,0:T(2,128)(2,1)S(1)} %all-to-all-done) | data formatting | bytes 1966080
  149.5 8.4 %copy.8 = bf16[1,60,8192]{2,1,0:T(8,128)(2,1)S(1)} copy(bf16[1,60,8192]{1,0,2:T(2,128)(2,1)} %bitcast.42) | data formatting | bytes 1966080 | tf_op jit(solution)/shard_map/all_to_all | solution.py:93
  157.9 3.5 %all_to_all.12 = bf16[1,60,128,64]{3,2,1,0:T(8,128)(2,1)} reshape(bf16[1,60,8192]{2,1,0:T(8,128)(2,1)S(1)} %copy.8) | data formatting | bytes 1966080 | tf_op jit(solution)/shard_map/all_to_all | solution.py:93
  161.4 4.7 %copy.9 = bf16[1,128,60,64]{2,1,3,0:T(8,128)(2,1)S(1)} copy(bf16[1,128,60,64]{3,1,2,0:T(8,128)(2,1)} %bitcast.43) | data formatting | bytes 1966080 | tf_op jit(solution)/shard_map/all_to_all | solution.py:93
  166.1 4.1 %reshape.141 = bf16[7680,64]{0,1:T(8,128)(2,1)S(1)} reshape(bf16[1,128,60,64]{2,1,3,0:T(8,128)(2,1)S(1)} %copy.9) | data formatting | bytes 1966080 | tf_op jit(solution)/shard_map/reshape
  170.2 5.6 %fusion.2 = f32[768,64]{0,1:T(8,128)S(1)} fusion(bf16[7680,64]{0,1:T(8,128)(2,1)S(1)} %reshape.141, bf16[7680,384]{1,0:T(8,128)(2,1)} %get-tuple-element.12, bf16[7680,384]{1,0:T(8,128)(2,1)} %get-tuple-element.11), kind=kOutput, calls=%fused_computation.3 | convolution fusion | flops 778567680 | bytes 12976128 | tf_op jit(solution)/shard_map/nta,tf->naf/dot_general | solution.py:91
  175.8 0.7 fusion.20
  176.5 0.1 fusion.35
  176.6 1.3 collective-permute-start.1
  177.9 3.9 %collective-permute-start = (bf16[1,64,768]{2,1,0:T(8,128)(2,1)S(1)}, bf16[1,64,768]{2,1,0:T(8,128)(2,1)S(1)}, u32[]{:S(2)}, u32[]{:S(2)}) collective-permute-start(bf16[1,64,768]{2,1,0:T(8,128)(2,1)S(1)} %bitcast.46), channel_id=1, source_target_pairs={{1,0},{2,1},{3,2},{4,3},{5,4},{6,5},{7,6},{8,7},{9,8},{10,9},{11,1... | collective-permute-start | bytes 294920 | tf_op jit(solution)/shard_map/ppermute | solution.py:18
  181.8 0.3 fusion.46
  182.1 0.0 collective-permute-done.1
  182.1 4.0 %collective-permute-done = bf16[1,64,768]{2,1,0:T(8,128)(2,1)S(1)} collective-permute-done((bf16[1,64,768]{2,1,0:T(8,128)(2,1)S(1)}, bf16[1,64,768]{2,1,0:T(8,128)(2,1)S(1)}, u32[]{:S(2)}, u32[]{:S(2)}) %collective-permute-start) | collective-permute-done | bytes 98336 | tf_op jit(solution)/shard_map/ppermute | solution.py:18
  186.2 2.6 %add_convert_fusion = (bf16[192,32,384]{2,1,0:T(8,128)(2,1)S(1)}, bf16[192,32,384]{2,1,0:T(8,128)(2,1)S(1)}) fusion(f32[32,384]{1,0:T(8,128)S(1)} %get-tuple-element.10, f32[192,384]{1,0:T(8,128)S(1)} %get-tuple-element.8, f32[32,384]{1,0:T(8,128)S(1)} %get-tuple-element.9, f32[192,384]{1,0:T(8,128)S(1)} %get-tuple-element.7), kind=kLoop, calls=%fused_computation.18 | loop fusion | flops 18874368 | bytes 10125312 | tf_op jit(solution)/shard_map/convert.9
  188.8 2.9 %fusion.16 = bf16[32,64,192]{1,0,2:T(8,128)(2,1)S(1)} fusion(bf16[192,32,384]{2,1,0:T(8,128)(2,1)S(1)} %get-tuple-element.6, bf16[192,32,384]{2,1,0:T(8,128)(2,1)S(1)} %get-tuple-element.5, bf16[64,768]{1,0:T(8,128)(2,1)S(1)} %fusion.35), kind=kOutput, calls=%fused_computation.20 | convolution fusion | flops 623247360 | bytes 10321920 | tf_op jit(solution)/shard_map/nak,nblk->lab/dot_general | solution.py:115
  191.7 0.0 copy-start.1
  191.7 0.0 copy-start.2
  191.7 1.4 copy.10
  193.1 1.1 reshape.143
  194.3 0.1 concatenate.31
  194.3 3.2 %reshape.144 = bf16[32,64,193]{2,1,0:T(8,128)(2,1)S(1)} reshape(bf16[32,12352]{1,0:T(8,128)(2,1)S(1)} %concatenate.31) | data formatting | bytes 1581056 | tf_op jit(solution)/shard_map/vmap()/reshape | solution.py:71
  197.5 0.9 slice_bitcast_fusion
  198.4 0.0 all-gather.3.cloned.1.call-update
  198.4 1.3 collective-permute-start.3
  199.7 1.9 collective-permute-start.2
  201.7 1.1 collective-permute-done.3
  202.8 1.9 collective-permute-done.2
  204.6 0.2 convolution_bitcast_fusion
  204.8 0.1 reshape.145
  205.0 0.2 reshape.146
  205.2 0.0 copy-done.1
  205.2 0.0 copy-done.2
  205.2 0.1 fusion.50
  205.3 30.2 %all-gather.3.cloned.1.call-done = bf16[256,32,128]{2,0,1:T(8,128)(2,1)} async-done(((bf16[64,32,128]{2,0,1:T(8,128)(2,1)}), bf16[256,32,128]{2,0,1:T(8,128)(2,1)}) %all-gather.3.cloned.1.call-update) | async-done | bytes 2097168 | tf_op jit(solution)/shard_map/all_gather | solution.py:117
  235.5 2.0 reduce_sum.12
  237.5 0.1 convert_multiply_fusion
  237.6 1.6 copy.11
  (7 shorter events, 0.1 us)
Async XLA Ops:
  15.7 72.9 %copy-start = (s32[4,64]{1,0:T(4,128)S(1)}, s32[4,64]{1,0:T(4,128)}, u32[]{:S(2)}) copy-start(s32[4,64]{1,0:T(4,128)} %param.5) | copy-start | bytes 3076
  67.9 72.2 %all-to-all-start = ((bf16[128,2,1920]{2,1,0:T(2,128)(2,1)}), bf16[128,2,1920]{2,1,0:T(2,128)(2,1)S(1)}, u32[]{:S(2)}, u32[]{:S(2)}) async-start(bf16[128,2,1920]{2,1,0:T(2,128)(2,1)} %reshape.151), calls=%async_computation | async-start | bytes 1966080 | tf_op jit(solution)/shard_map/all_to_all | solution.py:93
  88.4 147.0 %all-gather.3.cloned.1.call-start = ((), (), s32[]{:S(2)}) async-start(), calls=%async_computation.1 | async-start | bytes 2621440 | tf_op jit(solution)/shard_map/all_gather | solution.py:117
  176.6 5.5 %collective-permute-start.1 = (bf16[1,64,768]{2,1,0:T(8,128)(2,1)S(1)}, bf16[1,64,768]{2,1,0:T(8,128)(2,1)S(1)}, u32[]{:S(2)}, u32[]{:S(2)}) collective-permute-start(bf16[1,64,768]{2,1,0:T(8,128)(2,1)S(1)} %bitcast.45), channel_id=1, source_target_pairs={{2,0},{3,1},{4,2},{5,3},{6,4},{7,5},{8,6},{9,7},{10,8},{11,9},{12,... | collective-permute-start | bytes 294920 | tf_op jit(solution)/shard_map/ppermute | solution.py:18
  177.9 8.2 %collective-permute-start = (bf16[1,64,768]{2,1,0:T(8,128)(2,1)S(1)}, bf16[1,64,768]{2,1,0:T(8,128)(2,1)S(1)}, u32[]{:S(2)}, u32[]{:S(2)}) collective-permute-start(bf16[1,64,768]{2,1,0:T(8,128)(2,1)S(1)} %bitcast.46), channel_id=1, source_target_pairs={{1,0},{2,1},{3,2},{4,3},{5,4},{6,5},{7,6},{8,7},{9,8},{10,9},{11,1... | collective-permute-start | bytes 294920 | tf_op jit(solution)/shard_map/ppermute | solution.py:18
  191.7 13.5 %copy-start.1 = (s32[64]{0:T(128)S(1)}, s32[64]{0:T(128)}, u32[]{:S(2)}) copy-start(s32[64]{0:T(128)} %param.7) | copy-start | bytes 772
  191.7 13.5 %copy-start.2 = (s32[64]{0:T(128)S(1)}, s32[64]{0:T(128)}, u32[]{:S(2)}) copy-start(s32[64]{0:T(128)} %param.6) | copy-start | bytes 772
  198.4 4.3 %collective-permute-start.3 = (bf16[4,64]{1,0:T(4,128)(2,1)S(1)}, bf16[4,64]{1,0:T(4,128)(2,1)S(1)}, u32[]{:S(2)}, u32[]{:S(2)}) collective-permute-start(bf16[4,64]{1,0:T(4,128)(2,1)S(1)} %convert_element_type.47), channel_id=1, source_target_pairs={{2,0},{3,1},{4,2},{5,3},{6,4},{7,5},{8,6},{9,7},{10,8},{11,9},{12,... | collective-permute-start | bytes 1544 | tf_op jit(solution)/shard_map/ppermute | solution.py:18
  199.7 4.9 %collective-permute-start.2 = (bf16[4,64]{1,0:T(4,128)(2,1)S(1)}, bf16[4,64]{1,0:T(4,128)(2,1)S(1)}, u32[]{:S(2)}, u32[]{:S(2)}) collective-permute-start(bf16[4,64]{1,0:T(4,128)(2,1)S(1)} %convert_element_type.47), channel_id=1, source_target_pairs={{1,0},{2,1},{3,2},{4,3},{5,4},{6,5},{7,6},{8,7},{9,8},{10,9},{11,1... | collective-permute-start | bytes 1544 | tf_op jit(solution)/shard_map/ppermute | solution.py:18
Sparse Core Ops, SparseCore 0:
  198.6 36.8 all-gather.2
